TPU v7x, 256 devices: a whole 4x4x8 slice. The times are simulated.
256 devices in a mesh: seq: 8 (over x_hi, y), exp: 32 (over x_lo, z, core).
Axes of the slice: x: 4 (x_hi: 2, x_lo: 2; x = x_hi * 2 + x_lo), y: 4, z: 8, core: 2. Of those that a mesh axis runs over, the one named last changes fastest.
Arguments:
- tokens: bfloat16 [8192, 2560], P('exp'), may hold values from -6 to 6
- norm_gain: float32 [2560], replicated, may hold values from 0.1 to 1.9
- routes: int32 [8192, 6], P('exp'), may hold values from 0 to 63, all different within a row; in each aligned block of 256 rows (0 to 255, 256 to 511, ...) at most 25 rows name the same one
- route_weights: bfloat16 [8192, 6], P('exp'), may hold values from 0.049804688 to 0.3984375
- w_gate: bfloat16 [64, 2560, 1536], P('exp', None, 'seq'), may hold values from -0.125 to 0.125
- w_up: bfloat16 [64, 2560, 1536], P('exp', None, 'seq'), may hold values from -0.125 to 0.125
- w_down: bfloat16 [64, 1536, 2560], P('exp', 'seq'), may hold values from -0.15625 to 0.15625
- kv_prefill: bfloat16 [4, 2048, 32, 1024], P(None, ('seq', 'exp')), may hold values from -6 to 6
- block_map: int32 [2048], P(('seq', 'exp')), may hold values from 0 to 2047, as said below
- block_empty: int32 [2048], P(('seq', 'exp')), may hold values 0 or 1
Outputs:
- moe_out: bfloat16 [8192, 2560], P('exp', 'seq')
- kv_decode: bfloat16 [4, 2048, 32, 1024], P(None, ('seq', 'exp'))
Inputs may be any that keep to these rules, and one draw needn't show every extreme that they name: `routes`: in each aligned block of 256 rows no expert is named by more than 25 rows, a bound that some block reaches. block_map is a permutation of the 2048 blocks; a block keeps its index of exp, and each device sends exactly 1 block to each device of its seq group, itself included.
All inputs are finite; a program needn't handle non-finite values. No bound on the sum of `block_empty` on one device may be relied on, other than what follows from the above.
Results may differ from a plain program's by a relative error of at most 0.013.
Values may be sent and summed in bfloat16 or wider, within the bound.
No kernel may reach another device: no remote copies, remote signals or barrier semaphores. Data moves between devices by JAX's collectives and lax.ppermute only.
A program may use at most 128 MiB of HBM per device.

v0:
```python
import jax
import jax.numpy as jnp
from jax import lax
from jax.sharding import PartitionSpec as P


def passed_along(block, axis, distance):
    devices = range(lax.axis_size(axis))
    route = [((i - distance) % len(devices), i) for i in devices]
    return lax.ppermute(block, axis, route)


def rms_normed(tokens, norm_gain):
    values = tokens.astype(jnp.float32)
    scale = lax.rsqrt(jnp.mean(values * values, axis=-1, keepdims=True) + 1e-06)
    return (values * scale * norm_gain).astype(jnp.bfloat16)


def slot_layout(routes, experts, local_experts, owners, capacity):
    flat_routes = routes.reshape(-1)
    onehot = (flat_routes[:, None] == jnp.arange(experts, dtype=jnp.int32)[None, :]).astype(
        jnp.int32
    )
    before = jnp.cumsum(onehot, axis=0) - onehot
    position = jnp.sum(before * onehot, axis=1)
    owner = flat_routes // local_experts
    local_index = flat_routes % local_experts
    return (local_index * owners + owner) * capacity + position


def fill_slots(normed, slot_index, total_slots, topk):
    row_count = normed.shape[0]
    token_of = jnp.arange(slot_index.shape[0], dtype=jnp.int32) // topk
    source = jnp.full((total_slots,), row_count, jnp.int32).at[slot_index].set(token_of)
    padded = jnp.concatenate([normed, jnp.zeros((1, normed.shape[1]), normed.dtype)], axis=0)
    return padded[source]


def expert_block(rows, w_gate, w_up, w_down):
    gate = jnp.einsum("erd,edf->erf", rows, w_gate, preferred_element_type=jnp.float32)
    upward = jnp.einsum("erd,edf->erf", rows, w_up, preferred_element_type=jnp.float32)
    hidden = (jax.nn.silu(gate) * upward).astype(jnp.bfloat16)
    return jnp.einsum("erf,efd->erd", hidden, w_down, preferred_element_type=jnp.float32).astype(
        jnp.bfloat16
    )


def relayout(kv_prefill, block_map, block_empty):
    layers, blocks, block_rows, kv_width = kv_prefill.shape
    seq_count = lax.axis_size("seq")
    exp_count = lax.axis_size("exp")
    per_peer = blocks // seq_count
    keep = (1 - block_empty).astype(jnp.bfloat16)
    kept = kv_prefill * keep[None, :, None, None]
    peer = block_map // blocks // exp_count
    target = block_map % blocks
    order = jnp.argsort(peer * blocks + jnp.arange(blocks, dtype=jnp.int32))
    outgoing = kept[:, order].reshape(layers, seq_count, per_peer, block_rows, kv_width)
    labels = target[order].astype(jnp.bfloat16).reshape(1, seq_count, per_peer)
    my_seq = lax.axis_index("seq")
    arrived = outgoing
    tags = labels
    for step in range(1, seq_count):
        ahead = (my_seq + step) % seq_count
        piece = lax.dynamic_slice_in_dim(outgoing, ahead, 1, 1)
        label = lax.dynamic_slice_in_dim(labels, ahead, 1, 1)
        piece, label = passed_along((piece, label), "seq", step)
        behind = (my_seq - step + seq_count) % seq_count
        arrived = lax.dynamic_update_slice_in_dim(arrived, piece, behind, 1)
        tags = lax.dynamic_update_slice_in_dim(tags, label, behind, 1)
    arrived = arrived.reshape(layers, blocks, block_rows, kv_width)
    slots = tags.reshape(blocks).astype(jnp.int32)
    return arrived[:, jnp.argsort(slots)]


def per_device(
    tokens,
    norm_gain,
    routes,
    route_weights,
    w_gate,
    w_up,
    w_down,
    kv_prefill,
    block_map,
    block_empty,
):
    local_experts = w_gate.shape[0]
    exp_count = lax.axis_size("exp")
    experts = local_experts * exp_count
    tok_count, topk = routes.shape
    capacity = tok_count * topk // experts + 1
    normed = rms_normed(tokens, norm_gain)
    width = normed.shape[1]
    slot_index = slot_layout(routes, experts, local_experts, exp_count, capacity)
    total_slots = local_experts * exp_count * capacity
    outgoing = fill_slots(normed, slot_index, total_slots, topk).reshape(
        local_experts, exp_count * capacity, width
    )
    arrived = lax.all_to_all(outgoing, "exp", split_axis=1, concat_axis=1, tiled=True)
    partial_value = expert_block(arrived, w_gate, w_up, w_down)
    weights = route_weights.astype(jnp.float32)[:, :, None]
    returned = lax.all_to_all(
        partial_value, "exp", split_axis=1, concat_axis=1, tiled=True
    ).reshape(total_slots, width)
    picked = returned[slot_index].astype(jnp.float32).reshape(tok_count, topk, width)
    terms = jnp.sum(picked * weights, axis=1)
    mixed = lax.psum_scatter(terms.astype(jnp.bfloat16), "seq", scatter_dimension=1, tiled=True)
    kv_decode = relayout(kv_prefill, block_map, block_empty)
    return (mixed, kv_decode)


def solution(mesh):
    in_specs = (
        P("exp", None),
        P(),
        P("exp", None),
        P("exp", None),
        P("exp", None, "seq"),
        P("exp", None, "seq"),
        P("exp", "seq", None),
        P(None, ("seq", "exp"), None, None),
        P(("seq", "exp")),
        P(("seq", "exp")),
    )
    out_specs = (P("exp", "seq"), P(None, ("seq", "exp"), None, None))
    return jax.shard_map(
        per_device, mesh=mesh, in_specs=in_specs, out_specs=out_specs, check_vma=False
    )
```

profile of v0, /device:TPU:120, one launch (start us, length us, event | category | flops | bytes accessed | tf_op | source)
XLA Modules:
  0.0 717.7 jit_solution(14914148657757064392)
XLA Ops:
  11.1 34.6 %reduce-window.6 = s32[64,12,128]{2,1,0:T(8,128)} reduce-window(s32[64,12,128]{2,1,0:T(8,128)} %fusion.16, s32[]{:T(128)} %constant.187.clone.1), window={size=1x1x128 pad=0_0x0_0x127_0}, to_apply=%region_1.0 | reduce-window | flops 12484608 | bytes 786436 | tf_op jit(solution)/shard_map/reduce-window
  50.7 6.2 scatter_custom_fusion
  57.4 8.3 %gather_fusion = bf16[1600,2560]{1,0:T(8,128)(2,1)} fusion(bf16[257,2560]{1,0:T(8,128)(2,1)S(1)} %concatenate.3, s32[2048]{0:T(1024)S(1)} %pad_clamp_fusion.1), kind=kCustom, calls=%fused_computation | custom fusion | bytes 16390400 | tf_op jit(solution)/shard_map/gather | solution.py:36
  65.7 37.7 %copy.47 = bf16[2,800,2560]{2,0,1:T(2,128)(2,1)S(1)} copy(bf16[2,800,2560]{2,1,0:T(8,128)(2,1)} %bitcast.71) | data formatting | bytes 16384000 | tf_op jit(solution)/shard_map/reshape | solution.py:97
  103.3 188.8 %all_to_all.10 = bf16[2,800,2560]{2,0,1:T(2,128)(2,1)S(1)} all-to-all(bf16[2,800,2560]{2,0,1:T(2,128)(2,1)S(1)} %copy.47), channel_id=1, replica_groups=mesh['seq'=8,'exp'=32] {'exp'}, dimensions={1} | all-to-all | bytes 16384000 | tf_op jit(solution)/shard_map/all_to_all | solution.py:100
  292.1 3.2 copy-done.2
  295.3 4.2 fusion.2
  299.5 14.7 %convolution_convert_fusion = bf16[2,800,2560]{2,1,0:T(8,128)(2,1)} fusion(bf16[2,192,2560]{2,1,0:T(8,128)(2,1)S(1)} %copy-done, bf16[2,2560,192]{1,2,0:T(8,128)(2,1)} %param.15, bf16[2,800,2560]{2,0,1:T(2,128)(2,1)} %copy-done.2, f32[2,800,192]{1,2,0:T(8,128)} %fusion.2), kind=kOutput, calls=%fused_computation.11 | convolution fusion | flops 3151667200 | bytes 21544960 | tf_op jit(solution)/shard_map/erf,efd->erd/dot_general | solution.py:43
  314.2 38.5 %copy.50 = bf16[2,800,2560]{2,0,1:T(2,128)(2,1)} copy(bf16[2,800,2560]{2,1,0:T(8,128)(2,1)} %convolution_convert_fusion) | data formatting | bytes 16384000 | tf_op jit(solution)/shard_map/convert_element_type | solution.py:43
  352.7 7.3 %all-to-all-start.1 = ((bf16[2,800,2560]{2,0,1:T(2,128)(2,1)}), bf16[2,800,2560]{2,0,1:T(2,128)(2,1)}, u32[]{:S(2)}, u32[]{:S(2)}) async-start(bf16[2,800,2560]{2,0,1:T(2,128)(2,1)} %copy.50), calls=%async_computation.1 | async-start | bytes 16384000 | tf_op jit(solution)/shard_map/all_to_all | solution.py:103
  361.4 182.3 %all-to-all-done.1 = bf16[2,800,2560]{2,0,1:T(2,128)(2,1)} async-done(((bf16[2,800,2560]{2,0,1:T(2,128)(2,1)}), bf16[2,800,2560]{2,0,1:T(2,128)(2,1)}, u32[]{:S(2)}, u32[]{:S(2)}) %all-to-all-start.1) | async-done | bytes 8192032 | tf_op jit(solution)/shard_map/all_to_all | solution.py:103
  543.7 7.8 %copy.51 = bf16[2,800,2560]{2,1,0:T(8,128)(2,1)} copy(bf16[2,800,2560]{2,0,1:T(2,128)(2,1)} %all-to-all-done.1) | data formatting | bytes 16384000 | tf_op jit(solution)/shard_map/all_to_all | solution.py:103
  551.5 19.5 %gather_fusion.1 = bf16[1536,2560]{1,0:T(8,128)(2,1)} fusion(bf16[1600,2560]{1,0:T(8,128)(2,1)} %bitcast.70, s32[2048]{0:T(1024)S(1)} %pad_clamp_fusion), kind=kCustom, calls=%fused_computation.1 | custom fusion | bytes 15734784 | tf_op jit(solution)/shard_map/gather | solution.py:106
  571.0 14.2 %reshape.261 = f32[256,6,2560]{2,1,0:T(8,128)} reshape(bf16[1536,2560]{1,0:T(8,128)(2,1)} %gather_fusion.1) | data formatting | bytes 23592960 | tf_op jit(solution)/shard_map/convert_element_type | solution.py:106
  585.2 11.4 %multiply_reduce_fusion = bf16[256,2560]{1,0:T(8,128)(2,1)S(1)} fusion(f32[256,6,2560]{2,1,0:T(8,128)} %reshape.261, f32[256,6]{1,0:T(8,128)S(1)} %copy.52), kind=kLoop, calls=%fused_computation.6 | loop fusion | flops 7208960 | bytes 17045504 | tf_op jit(solution)/shard_map/reduce_sum | solution.py:107
  598.2 3.1 broadcast_multiply_fusion
  601.3 3.6 gather_fusion.2
  611.7 2.7 collective-permute-start.3
  615.8 3.4 collective-permute-start.7
  619.2 22.8 %collective-permute-done.7 = bf16[1,1,1]{2,1,0:T(2,128)(2,1)} collective-permute-done((bf16[1,1,1]{2,1,0:T(2,128)(2,1)}, bf16[1,1,1]{2,1,0:T(2,128)(2,1)}, u32[]{:S(2)}, u32[]{:S(2)}) %collective-permute-start.7) | collective-permute-done | bytes 34 | tf_op jit(solution)/shard_map/ppermute | solution.py:10
  643.0 4.5 collective-permute-done.8
  647.4 3.4 collective-permute-start.9
  652.4 5.8 collective-permute-start.10
  659.7 4.4 collective-permute-start.11
  665.7 4.4 collective-permute-start.12
  676.3 4.5 collective-permute-done.13
  684.7 3.6 collective-permute-start.6
  691.1 4.0 collective-permute-done.5
  695.9 3.9 collective-permute-done.6
  700.5 3.2 copy.53
  703.7 3.6 gather_fusion.4
  707.3 3.3 copy.55
  (87 shorter events, 40.2 us)
Async XLA Ops:
  7.2 292.3 %copy-start = (bf16[2,192,2560]{2,1,0:T(8,128)(2,1)S(1)}, bf16[2,192,2560]{2,1,0:T(8,128)(2,1)}, u32[]{:S(2)}) copy-start(bf16[2,192,2560]{2,1,0:T(8,128)(2,1)} %param.16) | copy-start | bytes 5898244
  11.1 45.8 %copy-start.3 = (bf16[256,2560]{1,0:T(8,128)(2,1)S(1)}, bf16[256,2560]{1,0:T(8,128)(2,1)}, u32[]{:S(2)}) copy-start(bf16[256,2560]{1,0:T(8,128)(2,1)} %param.10) | copy-start | bytes 3932164
  11.1 45.8 %copy-start.4 = (f32[2560]{0:T(1024)S(1)}, f32[2560]{0:T(1024)}, u32[]{:S(2)}) copy-start(f32[2560]{0:T(1024)} %param.11) | copy-start | bytes 30724
  103.3 192.0 %copy-start.6 = (bf16[2,2560,192]{1,2,0:T(8,128)(2,1)S(1)}, bf16[2,2560,192]{1,2,0:T(8,128)(2,1)}, u32[]{:S(2)}) copy-start(bf16[2,2560,192]{1,2,0:T(8,128)(2,1)} %param.14) | copy-start | bytes 5898244
  292.1 3.2 copy-start.2
  352.7 7.6 %copy-start.5 = (bf16[256,6]{0,1:T(8,128)(2,1)S(1)}, bf16[256,6]{0,1:T(8,128)(2,1)}, u32[]{:S(2)}) copy-start(bf16[256,6]{0,1:T(8,128)(2,1)} %param.13) | copy-start | bytes 9220
  352.7 7.7 %copy-start.7 = (s32[8]{0:T(128)S(1)}, s32[8]{0:T(128)}, u32[]{:S(2)}) copy-start(s32[8]{0:T(128)} %param.18) | copy-start | bytes 100
  352.7 8.7 %copy-start.8 = (s32[8]{0:T(128)S(1)}, s32[8]{0:T(128)}, u32[]{:S(2)}) copy-start(s32[8]{0:T(128)} %param.19) | copy-start | bytes 100
  352.7 191.0 %all-to-all-start.1 = ((bf16[2,800,2560]{2,0,1:T(2,128)(2,1)}), bf16[2,800,2560]{2,0,1:T(2,128)(2,1)}, u32[]{:S(2)}, u32[]{:S(2)}) async-start(bf16[2,800,2560]{2,0,1:T(2,128)(2,1)} %copy.50), calls=%async_computation.1 | async-start | bytes 16384000 | tf_op jit(solution)/shard_map/all_to_all | solution.py:103
  360.0 350.6 %reduce-scatter.4.cloned.1.call-start = ((), (), s32[]{:S(2)}) async-start(), calls=%async_computation.3 | async-start | bytes 1474560
  606.6 76.1 %collective-permute-start = (bf16[4,1,1,32,1024]{4,3,0,2,1:T(8,128)(2,1)S(1)}, bf16[4,1,1,32,1024]{4,3,0,2,1:T(8,128)(2,1)S(1)}, u32[]{:S(2)}, u32[]{:S(2)}) collective-permute-start(bf16[4,1,1,32,1024]{4,3,0,2,1:T(8,128)(2,1)S(1)} %get-tuple-element.20), channel_id=1, source_target_pairs={{224,0},{0,32},{32,64},{64,96},{96,128},{128,160},{160,192},{192,2... | collective-permute-start | bytes 786440 | tf_op jit(solution)/shard_map/ppermute | solution.py:10
  609.0 75.6 %collective-permute-start.1 = (bf16[4,1,1,32,1024]{4,3,0,2,1:T(8,128)(2,1)S(1)}, bf16[4,1,1,32,1024]{4,3,0,2,1:T(8,128)(2,1)S(1)}, u32[]{:S(2)}, u32[]{:S(2)}) collective-permute-start(bf16[4,1,1,32,1024]{4,3,0,2,1:T(8,128)(2,1)S(1)} %get-tuple-element.19), channel_id=1, source_target_pairs={{192,0},{224,32},{0,64},{32,96},{64,128},{96,160},{128,192},{160,2... | collective-permute-start | bytes 786440 | tf_op jit(solution)/shard_map/ppermute | solution.py:10
  611.6 77.3 %collective-permute-start.2 = (bf16[4,1,1,32,1024]{4,3,0,2,1:T(8,128)(2,1)S(1)}, bf16[4,1,1,32,1024]{4,3,0,2,1:T(8,128)(2,1)S(1)}, u32[]{:S(2)}, u32[]{:S(2)}) collective-permute-start(bf16[4,1,1,32,1024]{4,3,0,2,1:T(8,128)(2,1)S(1)} %get-tuple-element.18), channel_id=1, source_target_pairs={{160,0},{192,32},{224,64},{0,96},{32,128},{64,160},{96,192},{128,2... | collective-permute-start | bytes 786440 | tf_op jit(solution)/shard_map/ppermute | solution.py:10
  611.7 78.0 %collective-permute-start.3 = (bf16[4,1,1,32,1024]{4,3,0,2,1:T(8,128)(2,1)S(1)}, bf16[4,1,1,32,1024]{4,3,0,2,1:T(8,128)(2,1)S(1)}, u32[]{:S(2)}, u32[]{:S(2)}) collective-permute-start(bf16[4,1,1,32,1024]{4,3,0,2,1:T(8,128)(2,1)S(1)} %get-tuple-element.17), channel_id=1, source_target_pairs={{128,0},{160,32},{192,64},{224,96},{0,128},{32,160},{64,192},{96,2... | collective-permute-start | bytes 786440 | tf_op jit(solution)/shard_map/ppermute | solution.py:10
  615.8 26.2 %collective-permute-start.7 = (bf16[1,1,1]{2,1,0:T(2,128)(2,1)}, bf16[1,1,1]{2,1,0:T(2,128)(2,1)}, u32[]{:S(2)}, u32[]{:S(2)}) collective-permute-start(bf16[1,1,1]{2,1,0:T(2,128)(2,1)} %bitcast.19), channel_id=1, source_target_pairs={{224,0},{0,32},{32,64},{64,96},{96,128},{128,160},{160,192},{192,2... | collective-permute-start | bytes 14 | tf_op jit(solution)/shard_map/ppermute | solution.py:10
  642.0 5.4 collective-permute-start.8
  647.4 4.9 collective-permute-start.9
  652.4 7.4 %collective-permute-start.10 = (bf16[1,1,1]{2,1,0:T(2,128)(2,1)}, bf16[1,1,1]{2,1,0:T(2,128)(2,1)}, u32[]{:S(2)}, u32[]{:S(2)}) collective-permute-start(bf16[1,1,1]{2,1,0:T(2,128)(2,1)} %bitcast.25), channel_id=1, source_target_pairs={{128,0},{160,32},{192,64},{224,96},{0,128},{32,160},{64,192},{96,2... | collective-permute-start | bytes 14 | tf_op jit(solution)/shard_map/ppermute | solution.py:10
  659.7 6.0 collective-permute-start.11
  665.7 7.6 %collective-permute-start.12 = (bf16[1,1,1]{2,1,0:T(2,128)(2,1)}, bf16[1,1,1]{2,1,0:T(2,128)(2,1)}, u32[]{:S(2)}, u32[]{:S(2)}) collective-permute-start(bf16[1,1,1]{2,1,0:T(2,128)(2,1)} %bitcast.29), channel_id=1, source_target_pairs={{64,0},{96,32},{128,64},{160,96},{192,128},{224,160},{0,192},{32,2... | collective-permute-start | bytes 14 | tf_op jit(solution)/shard_map/ppermute | solution.py:10
  673.4 7.4 %collective-permute-start.13 = (bf16[1,1,1]{2,1,0:T(2,128)(2,1)}, bf16[1,1,1]{2,1,0:T(2,128)(2,1)}, u32[]{:S(2)}, u32[]{:S(2)}) collective-permute-start(bf16[1,1,1]{2,1,0:T(2,128)(2,1)} %bitcast.31), channel_id=1, source_target_pairs={{32,0},{64,32},{96,64},{128,96},{160,128},{192,160},{224,192},{0,2... | collective-permute-start | bytes 14 | tf_op jit(solution)/shard_map/ppermute | solution.py:10
  680.8 9.6 %collective-permute-start.4 = (bf16[4,1,1,32,1024]{4,3,0,2,1:T(8,128)(2,1)S(1)}, bf16[4,1,1,32,1024]{4,3,0,2,1:T(8,128)(2,1)S(1)}, u32[]{:S(2)}, u32[]{:S(2)}) collective-permute-start(bf16[4,1,1,32,1024]{4,3,0,2,1:T(8,128)(2,1)S(1)} %get-tuple-element.16), channel_id=1, source_target_pairs={{96,0},{128,32},{160,64},{192,96},{224,128},{0,160},{32,192},{64,2... | collective-permute-start | bytes 786440 | tf_op jit(solution)/shard_map/ppermute | solution.py:10
  682.7 12.5 %collective-permute-start.5 = (bf16[4,1,1,32,1024]{4,3,0,2,1:T(8,128)(2,1)S(1)}, bf16[4,1,1,32,1024]{4,3,0,2,1:T(8,128)(2,1)S(1)}, u32[]{:S(2)}, u32[]{:S(2)}) collective-permute-start(bf16[4,1,1,32,1024]{4,3,0,2,1:T(8,128)(2,1)S(1)} %get-tuple-element.15), channel_id=1, source_target_pairs={{64,0},{96,32},{128,64},{160,96},{192,128},{224,160},{0,192},{32,2... | collective-permute-start | bytes 786440 | tf_op jit(solution)/shard_map/ppermute | solution.py:10
  684.7 15.1 %collective-permute-start.6 = (bf16[4,1,1,32,1024]{4,3,0,2,1:T(8,128)(2,1)S(1)}, bf16[4,1,1,32,1024]{4,3,0,2,1:T(8,128)(2,1)S(1)}, u32[]{:S(2)}, u32[]{:S(2)}) collective-permute-start(bf16[4,1,1,32,1024]{4,3,0,2,1:T(8,128)(2,1)S(1)} %get-tuple-element.14), channel_id=1, source_target_pairs={{32,0},{64,32},{96,64},{128,96},{160,128},{192,160},{224,192},{0,2... | collective-permute-start | bytes 786440 | tf_op jit(solution)/shard_map/ppermute | solution.py:10
  707.3 3.3 copy-start.1
Sparse Core Ops, SparseCore 0:
  598.2 89.1 reduce-scatter.3
where the time goes:
time: 727 us; the launch traced here: 718 us
  waiting for transfers between devices  227 us (31%)
  blocking collectives  189 us (26%)
  local copies, waits for them, and re-layouts  169 us (23%)
  other arithmetic  55.6 us (8%)
  starting transfers between devices  44.2 us (6%)
  matrix products  18.9 us (3%)
  between operations  14.6 us (2%)
    all_to_all x1, blocking collectives, per_device(): lax.all_to_all(outgoing, 'exp', split_axis=1, concat_axis=1, tiled=True)  189 us
    all_to_all x1, waiting for transfers between devices, per_device(): lax.all_to_all(partial_value, 'exp', split_axis=1, concat_axis=1, tiled=T...  182 us
    ppermute x14, waiting for transfers between devices, passed_along(): return lax.ppermute(block, axis, route)  44.5 us
    convert_element_type x1, local copies, waits for them, and re-layouts, expert_block(): jnp.einsum('erf,efd->erd', hidden, w_down, preferred_element_type=jnp.flo...  38.5 us
    reshape x1, local copies, waits for them, and re-layouts, per_device(): fill_slots(normed, slot_index, total_slots, topk)  37.7 us
    ppermute x14, starting transfers between devices, passed_along(): return lax.ppermute(block, axis, route)  36.7 us
    another operation x3, other arithmetic  35.9 us
    gather x1, local copies, waits for them, and re-layouts, per_device(): returned[slot_index].astype(jnp.float32).reshape(tok_count, topk, width)  19.5 us
  transfers between devices with their start and end apart: 16, of which 10 were waited for; matrix products, arithmetic and copies ran while one was open for 4% of the time, Pallas kernels for 0%

commit v1 on v0

--- a/solution.py
+++ b/solution.py
@@ -100,9 +100,15 @@
     arrived = lax.all_to_all(outgoing, "exp", split_axis=1, concat_axis=1, tiled=True)
     partial_value = expert_block(arrived, w_gate, w_up, w_down)
     weights = route_weights.astype(jnp.float32)[:, :, None]
-    returned = lax.all_to_all(
-        partial_value, "exp", split_axis=1, concat_axis=1, tiled=True
-    ).reshape(total_slots, width)
+
+    def begin_the_shifts_all(local_block, mesh_ax, axis_no, d_out):
+        heard = lax.axis_size(mesh_ax)
+        later = jnp.stack(jnp.split(local_block, heard, axis=axis_no))
+        shaped = lax.all_to_all(later, mesh_ax, 0, 0)
+        formed = jnp.concatenate(shaped, axis=d_out)
+        return formed
+
+    returned = begin_the_shifts_all(partial_value, "exp", 1, 1).reshape(total_slots, width)
     picked = returned[slot_index].astype(jnp.float32).reshape(tok_count, topk, width)
     terms = jnp.sum(picked * weights, axis=1)
     mixed = lax.psum_scatter(terms.astype(jnp.bfloat16), "seq", scatter_dimension=1, tiled=True)

time: 727 us -> 703 us (0.967)
  other arithmetic: 55.6 us -> 38.5 us
    convert_element_type x1 -> x0, local copies, waits for them, and re-layouts: 38.5 us -> none  [expert_block(): jnp.einsum('erf,efd->erd', hidden, w_down, preferred_element_type=jnp.flo...]
    another operation x1 -> x4, local copies, waits for them, and re-layouts: 0.1 us -> 18.4 us  [the longest x1 10.4 us: per_device(): begin_the_shifts_all(partial_value, 'exp', 1, 1).reshape(total_slots, width)]
    another operation x3, other arithmetic: 35.9 us -> 18.4 us
    unnamed x21 -> x50, local copies, waits for them, and re-layouts: 8.98 us -> 24.6 us
    reshape x0 -> x1, local copies, waits for them, and re-layouts: none -> 9.53 us  [begin_the_shifts_all(): formed = jnp.concatenate(shaped, axis=d_out)]
    all_to_all x1 -> x0, local copies, waits for them, and re-layouts: 7.78 us -> none  [per_device(): lax.all_to_all(partial_value, 'exp', split_axis=1, concat_axis=1, tiled=T...]
  transfers between devices with their start and end apart: 16 -> 16, of which waited for: 10 -> 10; matrix products, arithmetic and copies ran while one was open for 4% -> 5% of each run, Pallas kernels for 0% -> 0%
where the time goes in v1:
time: 703 us; the launch traced here: 695 us
  waiting for transfers between devices  227 us (32%)
  blocking collectives  189 us (27%)
  local copies, waits for them, and re-layouts  164 us (23%)
  starting transfers between devices  43.9 us (6%)
  other arithmetic  38.5 us (5%)
  matrix products  18.8 us (3%)
  between operations  14.8 us (2%)
    all_to_all x1, blocking collectives, per_device(): lax.all_to_all(outgoing, 'exp', split_axis=1, concat_axis=1, tiled=True)  189 us
    all_to_all x1, waiting for transfers between devices, begin_the_shifts_all(): shaped = lax.all_to_all(later, mesh_ax, 0, 0)  182 us
    ppermute x14, waiting for transfers between devices, passed_along(): return lax.ppermute(block, axis, route)  44.3 us
    reshape x1, local copies, waits for them, and re-layouts, per_device(): fill_slots(normed, slot_index, total_slots, topk)  37.7 us
    ppermute x14, starting transfers between devices, passed_along(): return lax.ppermute(block, axis, route)  36.3 us
    unnamed x50, local copies, waits for them, and re-layouts  24.6 us
    gather x1, local copies, waits for them, and re-layouts, per_device(): returned[slot_index].astype(jnp.float32).reshape(tok_count, topk, width)  19.5 us
    another operation x3, other arithmetic  18.4 us
  transfers between devices with their start and end apart: 16, of which 10 were waited for; matrix products, arithmetic and copies ran while one was open for 5% of the time, Pallas kernels for 0%

profile of v1, /device:TPU:120, one launch (start us, length us, event | category | flops | bytes accessed | tf_op | source)
XLA Modules:
  0.0 695.4 jit_solution(96313104337102624)
XLA Ops:
  8.6 18.1 %reduce-window.6 = s32[64,12,128]{2,1,0:T(8,128)S(1)} reduce-window(s32[64,12,128]{2,1,0:T(8,128)S(1)} %fusion.16, s32[]{:T(128)} %constant.187.clone.1), window={size=1x1x128 pad=0_0x0_0x127_0}, to_apply=%region_1.0 | reduce-window | flops 12484608 | bytes 786436 | tf_op jit(solution)/shard_map/reduce-window
  27.9 6.2 scatter_custom_fusion
  37.5 8.3 %gather_fusion = bf16[1600,2560]{1,0:T(8,128)(2,1)} fusion(bf16[257,2560]{1,0:T(8,128)(2,1)S(1)} %concatenate.3, s32[2048]{0:T(1024)S(1)} %get-tuple-element.31), kind=kCustom, calls=%fused_computation | custom fusion | bytes 16390400 | tf_op jit(solution)/shard_map/gather | solution.py:36
  45.8 37.7 %copy.49 = bf16[2,800,2560]{2,0,1:T(2,128)(2,1)S(1)} copy(bf16[2,800,2560]{2,1,0:T(8,128)(2,1)} %bitcast.198) | data formatting | bytes 16384000 | tf_op jit(solution)/shard_map/reshape | solution.py:97
  83.5 188.8 %all_to_all.10 = bf16[2,800,2560]{2,0,1:T(2,128)(2,1)S(1)} all-to-all(bf16[2,800,2560]{2,0,1:T(2,128)(2,1)S(1)} %copy.49), channel_id=1, replica_groups=mesh['seq'=8,'exp'=32] {'exp'}, dimensions={1} | all-to-all | bytes 16384000 | tf_op jit(solution)/shard_map/all_to_all | solution.py:100
  272.3 3.1 copy-done.3
  275.4 4.2 fusion.2
  279.6 14.6 %convolution_convert_fusion = bf16[2,800,2560]{2,1,0:T(8,128)(2,1)} fusion(bf16[2,192,2560]{2,1,0:T(8,128)(2,1)S(1)} %copy-done, bf16[2,2560,192]{1,2,0:T(8,128)(2,1)} %param.15, bf16[2,800,2560]{2,0,1:T(2,128)(2,1)} %copy-done.3, f32[2,800,192]{1,2,0:T(8,128)} %fusion.2), kind=kOutput, calls=%fused_computation.11 | convolution fusion | flops 3151667200 | bytes 21544960 | tf_op jit(solution)/shard_map/erf,efd->erd/dot_general | solution.py:43
  310.3 7.8 %copy.52 = bf16[32,2,25,2560]{3,1,2,0:T(2,128)(2,1)} copy(bf16[32,2,25,2560]{3,2,1,0:T(8,128)(2,1)S(1)} %fusion.20) | data formatting | bytes 16384000 | tf_op jit(solution)/shard_map/stack | solution.py:106
  318.2 7.3 %all-to-all-start.1 = ((bf16[32,2,25,2560]{3,1,2,0:T(2,128)(2,1)}), bf16[32,2,25,2560]{3,1,2,0:T(2,128)(2,1)}, u32[]{:S(2)}, u32[]{:S(2)}) async-start(bf16[32,2,25,2560]{3,1,2,0:T(2,128)(2,1)} %copy.52), calls=%async_computation.1 | async-start | bytes 16384000 | tf_op jit(solution)/shard_map/all_to_all | solution.py:107
  326.8 182.3 %all-to-all-done.1 = bf16[32,2,25,2560]{3,1,2,0:T(2,128)(2,1)} async-done(((bf16[32,2,25,2560]{3,1,2,0:T(2,128)(2,1)}), bf16[32,2,25,2560]{3,1,2,0:T(2,128)(2,1)}, u32[]{:S(2)}, u32[]{:S(2)}) %all-to-all-start.1) | async-done | bytes 8192032 | tf_op jit(solution)/shard_map/all_to_all | solution.py:107
  509.2 9.5 %copy.53 = bf16[2,32,25,2560]{3,2,1,0:T(8,128)(2,1)} copy(bf16[2,32,25,2560]{3,0,2,1:T(2,128)(2,1)} %bitcast.35) | data formatting | bytes 16384000 | tf_op jit(solution)/shard_map/reshape | solution.py:108
  518.7 10.4 %reshape_reshape.3 = bf16[1600,2560]{1,0:T(8,128)(2,1)} reshape(bf16[2,32,25,2560]{3,2,1,0:T(8,128)(2,1)} %copy.53) | data formatting | bytes 16384000 | tf_op jit(solution)/shard_map/reshape;reshape | solution.py:111
  529.1 19.5 %gather_fusion.1 = bf16[1536,2560]{1,0:T(8,128)(2,1)} fusion(bf16[1600,2560]{1,0:T(8,128)(2,1)} %reshape_reshape.3, s32[2048]{0:T(1024)S(1)} %get-tuple-element.30), kind=kCustom, calls=%fused_computation.1 | custom fusion | bytes 15734784 | tf_op jit(solution)/shard_map/gather | solution.py:112
  548.5 14.2 %reshape.261 = f32[256,6,2560]{2,1,0:T(8,128)} reshape(bf16[1536,2560]{1,0:T(8,128)(2,1)} %gather_fusion.1) | data formatting | bytes 23592960 | tf_op jit(solution)/shard_map/convert_element_type | solution.py:112
  562.8 11.4 %multiply_reduce_fusion = bf16[256,2560]{1,0:T(8,128)(2,1)S(1)} fusion(f32[256,6,2560]{2,1,0:T(8,128)} %reshape.261, f32[256,6]{1,0:T(8,128)S(1)} %copy.54), kind=kLoop, calls=%fused_computation.6 | loop fusion | flops 7208960 | bytes 17045504 | tf_op jit(solution)/shard_map/reduce_sum | solution.py:113
  575.8 3.1 broadcast_multiply_fusion
  578.9 3.6 gather_fusion.2
  594.2 3.6 collective-permute-start.7
  597.8 21.8 %collective-permute-done.7 = bf16[1,1,1]{2,1,0:T(2,128)(2,1)} collective-permute-done((bf16[1,1,1]{2,1,0:T(2,128)(2,1)}, bf16[1,1,1]{2,1,0:T(2,128)(2,1)}, u32[]{:S(2)}, u32[]{:S(2)}) %collective-permute-start.7) | collective-permute-done | bytes 34 | tf_op jit(solution)/shard_map/ppermute | solution.py:10
  620.4 4.6 collective-permute-done.8
  625.0 3.3 collective-permute-start.9
  630.0 5.7 collective-permute-start.10
  637.4 4.4 collective-permute-start.11
  643.5 4.4 collective-permute-start.12
  653.8 4.6 collective-permute-done.13
  662.3 3.6 collective-permute-start.6
  668.8 4.0 collective-permute-done.5
  673.6 4.0 collective-permute-done.6
  678.3 3.2 copy.55
  681.5 3.6 gather_fusion.4
  685.1 3.2 copy.57
  (117 shorter events, 56.2 us)
Async XLA Ops:
  7.2 272.4 %copy-start = (bf16[2,192,2560]{2,1,0:T(8,128)(2,1)S(1)}, bf16[2,192,2560]{2,1,0:T(8,128)(2,1)}, u32[]{:S(2)}) copy-start(bf16[2,192,2560]{2,1,0:T(8,128)(2,1)} %param.16) | copy-start | bytes 5898244
  83.5 192.0 %copy-start.5 = (bf16[2,2560,192]{1,2,0:T(8,128)(2,1)S(1)}, bf16[2,2560,192]{1,2,0:T(8,128)(2,1)}, u32[]{:S(2)}) copy-start(bf16[2,2560,192]{1,2,0:T(8,128)(2,1)} %param.14) | copy-start | bytes 5898244
  272.3 3.2 copy-start.3
  294.2 14.5 %copy-start.2 = (bf16[2,800,2560]{2,1,0:T(8,128)(2,1)S(1)}, bf16[2,800,2560]{2,1,0:T(8,128)(2,1)}, u32[]{:S(2)}) copy-start(bf16[2,800,2560]{2,1,0:T(8,128)(2,1)} %convolution_convert_fusion) | copy-start | bytes 24576004
  318.2 7.5 %copy-start.4 = (bf16[256,6]{0,1:T(8,128)(2,1)S(1)}, bf16[256,6]{0,1:T(8,128)(2,1)}, u32[]{:S(2)}) copy-start(bf16[256,6]{0,1:T(8,128)(2,1)} %param.13) | copy-start | bytes 9220
  318.2 7.7 %copy-start.6 = (s32[8]{0:T(128)S(1)}, s32[8]{0:T(128)}, u32[]{:S(2)}) copy-start(s32[8]{0:T(128)} %param.18) | copy-start | bytes 100
  318.2 191.0 %all-to-all-start.1 = ((bf16[32,2,25,2560]{3,1,2,0:T(2,128)(2,1)}), bf16[32,2,25,2560]{3,1,2,0:T(2,128)(2,1)}, u32[]{:S(2)}, u32[]{:S(2)}) async-start(bf16[32,2,25,2560]{3,1,2,0:T(2,128)(2,1)} %copy.52), calls=%async_computation.1 | async-start | bytes 16384000 | tf_op jit(solution)/shard_map/all_to_all | solution.py:107
  325.5 362.9 %reduce-scatter.4.cloned.1.call-start = ((), (), s32[]{:S(2)}) async-start(), calls=%async_computation.3 | async-start | bytes 1474560
  562.8 12.9 %copy-start.7 = (s32[8]{0:T(128)S(1)}, s32[8]{0:T(128)}, u32[]{:S(2)}) copy-start(s32[8]{0:T(128)} %param.19) | copy-start | bytes 100
  585.1 75.3 %collective-permute-start = (bf16[4,1,1,32,1024]{4,3,0,2,1:T(8,128)(2,1)}, bf16[4,1,1,32,1024]{4,3,0,2,1:T(8,128)(2,1)S(1)}, u32[]{:S(2)}, u32[]{:S(2)}) collective-permute-start(bf16[4,1,1,32,1024]{4,3,0,2,1:T(8,128)(2,1)} %get-tuple-element.20), channel_id=1, source_target_pairs={{224,0},{0,32},{32,64},{64,96},{96,128},{128,160},{160,192},{192,2... | collective-permute-start | bytes 786440 | tf_op jit(solution)/shard_map/ppermute | solution.py:10
  587.5 74.8 %collective-permute-start.1 = (bf16[4,1,1,32,1024]{4,3,0,2,1:T(8,128)(2,1)}, bf16[4,1,1,32,1024]{4,3,0,2,1:T(8,128)(2,1)S(1)}, u32[]{:S(2)}, u32[]{:S(2)}) collective-permute-start(bf16[4,1,1,32,1024]{4,3,0,2,1:T(8,128)(2,1)} %get-tuple-element.19), channel_id=1, source_target_pairs={{192,0},{224,32},{0,64},{32,96},{64,128},{96,160},{128,192},{160,2... | collective-permute-start | bytes 786440 | tf_op jit(solution)/shard_map/ppermute | solution.py:10
  590.1 76.5 %collective-permute-start.2 = (bf16[4,1,1,32,1024]{4,3,0,2,1:T(8,128)(2,1)}, bf16[4,1,1,32,1024]{4,3,0,2,1:T(8,128)(2,1)S(1)}, u32[]{:S(2)}, u32[]{:S(2)}) collective-permute-start(bf16[4,1,1,32,1024]{4,3,0,2,1:T(8,128)(2,1)} %get-tuple-element.18), channel_id=1, source_target_pairs={{160,0},{192,32},{224,64},{0,96},{32,128},{64,160},{96,192},{128,2... | collective-permute-start | bytes 786440 | tf_op jit(solution)/shard_map/ppermute | solution.py:10
  590.2 77.2 %collective-permute-start.3 = (bf16[4,1,1,32,1024]{4,3,0,2,1:T(8,128)(2,1)}, bf16[4,1,1,32,1024]{4,3,0,2,1:T(8,128)(2,1)S(1)}, u32[]{:S(2)}, u32[]{:S(2)}) collective-permute-start(bf16[4,1,1,32,1024]{4,3,0,2,1:T(8,128)(2,1)} %get-tuple-element.17), channel_id=1, source_target_pairs={{128,0},{160,32},{192,64},{224,96},{0,128},{32,160},{64,192},{96,2... | collective-permute-start | bytes 786440 | tf_op jit(solution)/shard_map/ppermute | solution.py:10
  592.9 95.4 %copy-start.1 = (bf16[2,192,2560]{2,1,0:T(8,128)(2,1)S(1)}, bf16[2,192,2560]{2,1,0:T(8,128)(2,1)}, u32[]{:S(2)}) copy-start(bf16[2,192,2560]{2,1,0:T(8,128)(2,1)} %param.16) | copy-start | bytes 5898244
  594.2 25.4 %collective-permute-start.7 = (bf16[1,1,1]{2,1,0:T(2,128)(2,1)}, bf16[1,1,1]{2,1,0:T(2,128)(2,1)}, u32[]{:S(2)}, u32[]{:S(2)}) collective-permute-start(bf16[1,1,1]{2,1,0:T(2,128)(2,1)} %bitcast.51), channel_id=1, source_target_pairs={{224,0},{0,32},{32,64},{64,96},{96,128},{128,160},{160,192},{192,2... | collective-permute-start | bytes 14 | tf_op jit(solution)/shard_map/ppermute | solution.py:10
  619.6 5.4 collective-permute-start.8
  625.0 4.9 collective-permute-start.9
  630.0 7.4 %collective-permute-start.10 = (bf16[1,1,1]{2,1,0:T(2,128)(2,1)}, bf16[1,1,1]{2,1,0:T(2,128)(2,1)}, u32[]{:S(2)}, u32[]{:S(2)}) collective-permute-start(bf16[1,1,1]{2,1,0:T(2,128)(2,1)} %bitcast.57), channel_id=1, source_target_pairs={{128,0},{160,32},{192,64},{224,96},{0,128},{32,160},{64,192},{96,2... | collective-permute-start | bytes 14 | tf_op jit(solution)/shard_map/ppermute | solution.py:10
  637.4 6.1 collective-permute-start.11
  643.5 7.5 %collective-permute-start.12 = (bf16[1,1,1]{2,1,0:T(2,128)(2,1)}, bf16[1,1,1]{2,1,0:T(2,128)(2,1)}, u32[]{:S(2)}, u32[]{:S(2)}) collective-permute-start(bf16[1,1,1]{2,1,0:T(2,128)(2,1)} %bitcast.61), channel_id=1, source_target_pairs={{64,0},{96,32},{128,64},{160,96},{192,128},{224,160},{0,192},{32,2... | collective-permute-start | bytes 14 | tf_op jit(solution)/shard_map/ppermute | solution.py:10
  651.0 7.3 %collective-permute-start.13 = (bf16[1,1,1]{2,1,0:T(2,128)(2,1)}, bf16[1,1,1]{2,1,0:T(2,128)(2,1)}, u32[]{:S(2)}, u32[]{:S(2)}) collective-permute-start(bf16[1,1,1]{2,1,0:T(2,128)(2,1)} %bitcast.63), channel_id=1, source_target_pairs={{32,0},{64,32},{96,64},{128,96},{160,128},{192,160},{224,192},{0,2... | collective-permute-start | bytes 14 | tf_op jit(solution)/shard_map/ppermute | solution.py:10
  658.4 9.7 %collective-permute-start.4 = (bf16[4,1,1,32,1024]{4,3,0,2,1:T(8,128)(2,1)}, bf16[4,1,1,32,1024]{4,3,0,2,1:T(8,128)(2,1)S(1)}, u32[]{:S(2)}, u32[]{:S(2)}) collective-permute-start(bf16[4,1,1,32,1024]{4,3,0,2,1:T(8,128)(2,1)} %get-tuple-element.16), channel_id=1, source_target_pairs={{96,0},{128,32},{160,64},{192,96},{224,128},{0,160},{32,192},{64,2... | collective-permute-start | bytes 786440 | tf_op jit(solution)/shard_map/ppermute | solution.py:10
  660.5 12.4 %collective-permute-start.5 = (bf16[4,1,1,32,1024]{4,3,0,2,1:T(8,128)(2,1)}, bf16[4,1,1,32,1024]{4,3,0,2,1:T(8,128)(2,1)S(1)}, u32[]{:S(2)}, u32[]{:S(2)}) collective-permute-start(bf16[4,1,1,32,1024]{4,3,0,2,1:T(8,128)(2,1)} %get-tuple-element.15), channel_id=1, source_target_pairs={{64,0},{96,32},{128,64},{160,96},{192,128},{224,160},{0,192},{32,2... | collective-permute-start | bytes 786440 | tf_op jit(solution)/shard_map/ppermute | solution.py:10
  662.3 15.3 %collective-permute-start.6 = (bf16[4,1,1,32,1024]{4,3,0,2,1:T(8,128)(2,1)S(1)}, bf16[4,1,1,32,1024]{4,3,0,2,1:T(8,128)(2,1)S(1)}, u32[]{:S(2)}, u32[]{:S(2)}) collective-permute-start(bf16[4,1,1,32,1024]{4,3,0,2,1:T(8,128)(2,1)S(1)} %get-tuple-element.14), channel_id=1, source_target_pairs={{32,0},{64,32},{96,64},{128,96},{160,128},{192,160},{224,192},{0,2... | collective-permute-start | bytes 786440 | tf_op jit(solution)/shard_map/ppermute | solution.py:10
Sparse Core Ops, SparseCore 0:
  575.8 89.6 reduce-scatter.3
